TPU v7x, 32 devices: a whole 2x2x4 slice. The times are simulated.
32 devices in a mesh: dp: 8 (over z, core), ctx: 4 (over y, x).
Axes of the slice: x: 2, y: 2, z: 4, core: 2. Of those that a mesh axis runs over, the one named last changes fastest.
Arguments:
- hidden: bfloat16 [8, 512, 3072], P('dp', 'ctx'), may hold values from -6 to 6
- gating: bfloat16 [8, 512, 3072], P('dp', 'ctx'), may hold values from -6 to 6
- dt_raw: bfloat16 [8, 512, 48], P('dp', 'ctx'), may hold values from -4 to 4
- b_input: bfloat16 [8, 512, 128], P('dp', 'ctx'), may hold values from -0.5 to 0.5
- c_input: bfloat16 [8, 512, 128], P('dp', 'ctx'), may hold values from -0.5 to 0.5
- resets: int32 [8, 2], P('dp'), may hold values 0 or 1
- cotangent: bfloat16 [8, 512, 3072], P('dp', 'ctx'), may hold values from -18 to 18
- parameters: float32 [3216], replicated, may hold values from -10 to 2
- adam_mean: float32 [8, 804], P('dp'), may hold values from -6 to 6
- adam_square: float32 [8, 804], P('dp'), may hold values from 0.1 to 2
- bucket_size: int32 [8], replicated, may hold values from 1 to 804, 3216 in all
- bucket_owner: int32 [8], replicated, may hold values from 0 to 7, each once
Outputs:
- normed: bfloat16 [8, 512, 3072], P('dp', 'ctx')
- grad_hidden: bfloat16 [8, 512, 3072], P('dp', 'ctx')
- grad_gating: bfloat16 [8, 512, 3072], P('dp', 'ctx')
- grad_dt: bfloat16 [8, 512, 48], P('dp', 'ctx')
- grad_b: bfloat16 [8, 512, 128], P('dp', 'ctx')
- grad_c: bfloat16 [8, 512, 128], P('dp', 'ctx')
- new_params: float32 [3216], replicated
- new_mean: float32 [8, 804], P('dp')
- new_square: float32 [8, 804], P('dp')
Inputs may be any that keep to these rules, and one draw needn't show every extreme that they name: `bucket_size`: the sizes sum to 3216; the largest is exactly 804. `bucket_owner`: each dp index owns exactly one bucket.
All inputs are finite; a program needn't handle non-finite values. No bound on the sum of `resets` on one device may be relied on, other than what follows from the above.
Results may differ from a plain program's by a relative error of at most 0.0076.
Values may be sent and summed in bfloat16 or wider, within the bound.
No kernel may reach another device: no remote copies, remote signals or barrier semaphores. Data moves between devices by JAX's collectives and lax.ppermute only.
A program may use at most 128 MiB of HBM per device.

v0:
```python
import jax
import jax.numpy as jnp
from jax import lax
from jax.sharding import PartitionSpec as P

SPAN = 256
CH = 3072
eps_norm = 1e-05
clip_norm = 64.0
beta_one = 0.9
beta_two = 0.95
adam_eps = 1e-08
learn_rate = 0.02
step_count = 100.0
highest = lax.Precision.HIGHEST


def rounded(value):
    return lax.optimization_barrier(value.astype(jnp.bfloat16)).astype(jnp.float32)


def ssd_group(hidden, dt_raw, b_input, c_input, resets, a_log, dt_bias, skip):
    length = hidden.shape[0]
    heads = a_log.shape[0]
    width = hidden.shape[1] // heads
    blocks = length // SPAN
    step_sizes = jax.nn.softplus(dt_raw.astype(jnp.float32) + dt_bias)
    log_decay = (step_sizes * -jnp.exp(a_log)).reshape(blocks, SPAN, heads).transpose(0, 2, 1)
    cumul = jnp.cumsum(log_decay, axis=2)
    inputs = hidden.astype(jnp.float32).reshape(blocks, SPAN, heads, width)
    scaled = rounded(inputs * step_sizes.reshape(blocks, SPAN, heads, 1))
    b_rows = b_input.astype(jnp.float32).reshape(blocks, SPAN, -1)
    c_rows = c_input.astype(jnp.float32).reshape(blocks, SPAN, -1)
    scores = jnp.einsum("ctn,csn->cts", c_rows, b_rows, precision=highest)
    causal = jnp.arange(SPAN)[:, None] >= jnp.arange(SPAN)[None, :]
    spread = cumul[:, :, :, None] - cumul[:, :, None, :]
    decay = jnp.where(causal, jnp.exp(jnp.where(causal, spread, 0.0)), 0.0)
    weights = rounded(scores[:, None] * decay)
    intra = jnp.einsum("chts,cshp->cthp", weights, scaled, precision=highest)
    tail = cumul[:, :, -1:] - cumul
    b_decayed = rounded(b_rows[:, None] * jnp.exp(tail)[..., None])
    block_state = jnp.einsum("chsn,cshp->chnp", b_decayed, scaled, precision=highest)
    keep = 1.0 - resets.astype(jnp.float32)

    def advance(state, items):
        keep_one, total, added = items
        entering = state * keep_one
        return (jnp.exp(total)[:, None, None] * entering + added, entering)

    start_state = jnp.zeros(block_state.shape[1:], jnp.float32)
    last_state, entering = lax.scan(advance, start_state, (keep, cumul[:, :, -1], block_state))
    c_decayed = rounded(c_rows[:, None] * jnp.exp(cumul)[..., None])
    inter = jnp.einsum("chtn,chnp->cthp", c_decayed, rounded(entering), precision=highest)
    output = intra + inter + skip[:, None] * inputs
    return output.reshape(length, heads * width).astype(jnp.bfloat16)


def gate_values(y_values, gating):
    gated = y_values.astype(jnp.float32) * jax.nn.silu(gating.astype(jnp.float32))
    return (gated, jnp.sum(gated * gated, axis=-1))


def normalize(gated, total, gain):
    factor = lax.rsqrt(total / CH + eps_norm)
    return (factor, (gated * factor[..., None] * gain).astype(jnp.bfloat16))


def norm_backward(cotangent, gain, gated, factor, dot_total, y_values, gating):
    upstream = cotangent.astype(jnp.float32) * gain
    d_gated = (
        upstream * factor[..., None]
        - gated * (factor * factor * factor * dot_total / CH)[..., None]
    )
    gate_f = gating.astype(jnp.float32)
    sigma = jax.nn.sigmoid(gate_f)
    d_y = (d_gated * (gate_f * sigma)).astype(jnp.bfloat16)
    d_gate = (
        d_gated * y_values.astype(jnp.float32) * sigma * (1.0 + gate_f * (1.0 - sigma))
    ).astype(jnp.bfloat16)
    d_gain = jnp.sum(
        cotangent.astype(jnp.float32) * gated * factor[..., None], axis=tuple(range(gated.ndim - 1))
    )
    return (d_y, d_gate, d_gain)


def on_device(
    hidden,
    gating,
    dt_raw,
    b_input,
    c_input,
    resets,
    cotangent,
    parameters,
    adam_mean,
    adam_square,
    bucket_size,
    bucket_owner,
):
    heads_all = dt_raw.shape[2]
    groups = lax.axis_size("ctx")
    group = heads_all // groups
    state_size = b_input.shape[2]
    tokens = hidden.shape[1]
    first = lax.axis_index("ctx") * group
    head_params = parameters[: 3 * heads_all].reshape(3, heads_all)
    gain = parameters[3 * heads_all :]
    local_params = lax.dynamic_slice_in_dim(head_params, first, group, 1)
    b_all, c_all = (
        lax.all_gather(b_input, "ctx", axis=1, tiled=True),
        lax.all_gather(c_input, "ctx", axis=1, tiled=True),
    )
    seq_resets = resets[0]
    owners_n = lax.axis_size("dp")
    cap_n = adam_mean.shape[1]
    len_n = parameters.shape[0]
    state_all = lax.all_gather(jnp.stack([adam_mean[0], adam_square[0]]), "dp", axis=0)
    starts = jnp.cumsum(bucket_size) - bucket_size
    laid = jnp.zeros((2, len_n + cap_n), jnp.float32)
    for k in range(owners_n):
        laid = lax.dynamic_update_slice(laid, state_all[bucket_owner[k]], (0, starts[k]))
    mean_flat = laid[0, :len_n]
    square_flat = laid[1, :len_n]

    def local_fn(x_arg, dt_arg, b_arg, c_arg, a_arg, bias_arg, skip_arg):
        return ssd_group(x_arg, dt_arg, b_arg, c_arg, seq_resets, a_arg, bias_arg, skip_arg)

    x_heads, dt_heads = (
        lax.all_to_all(hidden, "ctx", split_axis=2, concat_axis=1, tiled=True),
        lax.all_to_all(dt_raw, "ctx", split_axis=2, concat_axis=1, tiled=True),
    )
    y_heads, pullback = jax.vjp(
        local_fn,
        x_heads[0],
        dt_heads[0],
        b_all[0],
        c_all[0],
        local_params[0],
        local_params[1],
        local_params[2],
    )
    y_seq = lax.all_to_all(y_heads[None], "ctx", split_axis=1, concat_axis=2, tiled=True)
    gated, total = gate_values(y_seq, gating)
    factor, normed = normalize(gated, total, gain)
    dot_total = jnp.sum(cotangent.astype(jnp.float32) * gain * gated, axis=-1)
    d_y, grad_gating, d_gain = norm_backward(
        cotangent, gain, gated, factor, dot_total, y_seq, gating
    )
    d_y_heads = lax.all_to_all(d_y, "ctx", split_axis=2, concat_axis=1, tiled=True)
    d_x, d_dt, d_b, d_c, d_alog, d_bias, d_skip = pullback(d_y_heads[0])
    d_pair = jnp.concatenate([d_b, d_c], axis=-1)
    grad_hidden, grad_dt, pair_parts = (
        lax.all_to_all(d_x[None], "ctx", split_axis=1, concat_axis=2, tiled=True),
        lax.all_to_all(d_dt[None], "ctx", split_axis=1, concat_axis=2, tiled=True),
        lax.all_to_all(d_pair[None], "ctx", split_axis=1, concat_axis=2, tiled=True),
    )
    pair_sum = jnp.sum(
        pair_parts.reshape(1, tokens, groups, 2 * state_size).astype(jnp.float32), axis=2
    ).astype(jnp.bfloat16)
    grad_b = pair_sum[..., :state_size]
    grad_c = pair_sum[..., state_size:]
    head_grads = jnp.stack([d_alog, d_bias, d_skip])
    full_heads = lax.dynamic_update_slice(
        jnp.zeros((3, heads_all), jnp.float32), head_grads, (0, first)
    )
    grad_part = jnp.concatenate([full_heads.reshape(-1), d_gain])
    gradient = lax.psum(grad_part, ("dp", "ctx"))
    grad_norm = jnp.sqrt(jnp.sum(gradient * gradient))
    shrink = jnp.minimum(1.0, clip_norm / (grad_norm + 1e-06))
    owners = lax.axis_size("dp")
    slot_cap = adam_mean.shape[1]
    total_len = parameters.shape[0]
    ends = jnp.cumsum(bucket_size)
    begins = ends - bucket_size
    order = jnp.arange(owners, dtype=jnp.int32)
    mine = lax.axis_index("dp")
    my_bucket = jnp.sum(jnp.where(bucket_owner == mine, order, 0))
    row_begin = jnp.sum(jnp.where(order == my_bucket, begins, 0))
    row_size = jnp.sum(jnp.where(order == my_bucket, bucket_size, 0))
    slots = jnp.arange(slot_cap, dtype=jnp.int32)
    valid = slots < row_size
    padding = jnp.zeros((slot_cap,), jnp.float32)
    grad_row = (
        jnp.where(
            valid,
            lax.dynamic_slice_in_dim(jnp.concatenate([gradient, padding]), row_begin, slot_cap),
            0.0,
        )
        * shrink
    )
    new_mean = beta_one * adam_mean[0] + (1.0 - beta_one) * grad_row
    new_square = beta_two * adam_square[0] + (1.0 - beta_two) * grad_row * grad_row
    grad_flat = gradient * shrink
    mean_all = beta_one * mean_flat + (1.0 - beta_one) * grad_flat
    square_all = beta_two * square_flat + (1.0 - beta_two) * grad_flat * grad_flat
    direction = (
        mean_all
        / (1.0 - beta_one**step_count)
        / (jnp.sqrt(square_all / (1.0 - beta_two**step_count)) + adam_eps)
    )
    new_params = parameters - learn_rate * direction
    return (
        normed,
        grad_hidden,
        grad_gating,
        grad_dt,
        grad_b,
        grad_c,
        new_params,
        new_mean[None],
        new_square[None],
    )


def solution(mesh):
    return jax.shard_map(
        on_device,
        mesh=mesh,
        in_specs=(
            P("dp", "ctx", None),
            P("dp", "ctx", None),
            P("dp", "ctx", None),
            P("dp", "ctx", None),
            P("dp", "ctx", None),
            P("dp", None),
            P("dp", "ctx", None),
            P(),
            P("dp", None),
            P("dp", None),
            P(),
            P(),
        ),
        out_specs=(
            P("dp", "ctx", None),
            P("dp", "ctx", None),
            P("dp", "ctx", None),
            P("dp", "ctx", None),
            P("dp", "ctx", None),
            P("dp", "ctx", None),
            P(),
            P("dp", None),
            P("dp", None),
        ),
        check_vma=False,
    )
```

profile of v0, /device:TPU:0, one launch (start us, length us, event | category | flops | bytes accessed | tf_op | source)
XLA Modules:
  0.0 367.2 jit_solution(14272552152918870720)
XLA Ops:
  3.3 5.2 %all-to-all-start.1 = ((bf16[4,2,768]{2,1,0:T(2,128)(2,1)}), bf16[4,2,768]{2,1,0:T(2,128)(2,1)S(1)}, u32[]{:S(2)}, u32[]{:S(2)}) async-start(bf16[4,2,768]{2,1,0:T(2,128)(2,1)} %reshape.560), calls=%async_computation.1 | async-start | bytes 24576 | tf_op jit(solution)/shard_map/all_to_all | solution.py:130
  10.6 9.1 %all_gather.13 = bf16[1,512,128]{2,1,0:T(8,128)(2,1)S(1)} all-gather(bf16[1,128,128]{2,1,0:T(8,128)(2,1)} %param.19), channel_id=1, replica_groups=mesh['dp'=8,'ctx'=4] {'ctx'}, dimensions={1}, use_global_device_ids=true | all-gather | bytes 163840 | tf_op jit(solution)/shard_map/all_gather | solution.py:110
  19.7 8.2 %all_gather.12 = bf16[1,512,128]{2,1,0:T(8,128)(2,1)S(1)} all-gather(bf16[1,128,128]{2,1,0:T(8,128)(2,1)} %param.20), channel_id=1, replica_groups=mesh['dp'=8,'ctx'=4] {'ctx'}, dimensions={1}, use_global_device_ids=true | all-gather | bytes 163840 | tf_op jit(solution)/shard_map/all_gather | solution.py:111
  28.7 3.8 %copy.220 = bf16[1,128,3072]{1,0,2:T(2,128)(2,1)S(1)} copy(bf16[1,128,3072]{2,1,0:T(8,128)(2,1)} %param.16) | data formatting | bytes 1572864 | tf_op args[0]
  32.5 17.9 %reduce.27 = bf16[3072,128]{1,0:T(8,128)(2,1)} reduce(bf16[3072,1,128]{2,1,0:T(2,128)(2,1)S(1)} %bitcast.223, bf16[]{:T(256)} %broadcast.249), dimensions={1}, to_apply=%bitcast.152.reduce_sub_computation | reduce | bytes 1572866
  50.4 2.0 reshape.562
  52.4 3.7 %all-to-all-start = ((bf16[4,2,49152]{2,1,0:T(2,128)(2,1)}), bf16[4,2,49152]{2,1,0:T(2,128)(2,1)S(1)}, u32[]{:S(2)}, u32[]{:S(2)}) async-start(bf16[4,2,49152]{2,1,0:T(2,128)(2,1)} %reshape.562), calls=%async_computation | async-start | bytes 1572864 | tf_op jit(solution)/shard_map/all_to_all | solution.py:129
  59.2 1.8 multiply_convert_fusion.2
  61.0 1.8 multiply_convert_fusion.1
  62.9 2.8 multiply_convert_fusion
  65.7 2.1 reshape.563
  67.7 3.2 bitcast_convert_fusion
  72.1 2.2 copy.221
  74.3 2.6 reshape.535
  78.9 1.8 fusion.88
  80.9 7.0 %while.36 = (s32[]{:T(128)}, f32[12,128,64]{2,1,0:T(8,128)S(1)}, f32[2,12,128,64]{3,2,1,0:T(8,128)S(1)}, f32[2,12]{1,0:T(2,128)S(1)}, f32[2,12,1,1]{1,3,2,0:T(1,...) while((s32[]{:T(128)}, f32[12,128,64]{2,1,0:T(8,128)S(1)}, ...), condition=%wide.region_3.4_spmd.clone, body=%wide.region_2.3_spmd.clone.sunk | while | flops 589827 | bytes 5899176 | solution.py:51
  88.1 2.5 fusion.89
  93.6 3.2 copy.238
  96.8 6.4 %reduce.28 = bf16[512,768]{1,0:T(8,128)(2,1)S(1)} reduce(bf16[512,1,768]{2,1,0:T(2,128)(2,1)} %bitcast.217, bf16[]{:T(256)} %broadcast.249), dimensions={1}, to_apply=%bitcast.154.reduce_sub_computation | reduce | bytes 1572866
  104.3 4.2 %all-to-all-start.2 = ((bf16[4,2,49152]{2,1,0:T(2,128)(2,1)}), bf16[4,2,49152]{2,1,0:T(2,128)(2,1)}, u32[]{:S(2)}, u32[]{:S(2)}) async-start(bf16[4,2,49152]{2,1,0:T(2,128)(2,1)} %reshape.564), calls=%async_computation.2 | async-start | bytes 1572864 | tf_op jit(solution)/shard_map/all_to_all | solution.py:142
  119.3 1.5 copy.241
  120.8 2.3 copy.242
  123.9 1.3 fusion.79
  125.3 3.7 %reshape.565 = bf16[512,1,768]{2,1,0:T(2,128)(2,1)} reshape(bf16[4,2,49152]{2,1,0:T(2,128)(2,1)} %all-to-all-done.2) | data formatting | bytes 1572864
  129.0 1.5 copy.239
  130.5 1.3 convert_bitcast_fusion
  131.8 3.0 copy.240
  134.9 2.0 multiply_reduce_fusion.1
  136.9 1.5 fusion.21
  138.4 2.5 fusion.30
  140.9 13.0 %copy.372 = bf16[1,128,3072]{1,0,2:T(2,128)(2,1)} copy(bf16[1,128,3072]{1,2,0:T(8,128)(2,1)S(1)} %get-tuple-element.489) | data formatting | bytes 1572864 | tf_op jit(solution)/shard_map/convert_element_type | solution.py:76
  153.9 18.5 %reduce.29 = bf16[3072,128]{1,0:T(8,128)(2,1)S(1)} reduce(bf16[3072,1,128]{2,1,0:T(2,128)(2,1)} %bitcast.219, bf16[]{:T(256)} %broadcast.249), dimensions={1}, to_apply=%bitcast.190.reduce_sub_computation | reduce | bytes 1572866
  173.4 4.1 %all-to-all-start.3 = ((bf16[4,2,49152]{2,1,0:T(2,128)(2,1)}), bf16[4,2,49152]{2,1,0:T(2,128)(2,1)S(1)}, u32[]{:S(2)}, u32[]{:S(2)}) async-start(bf16[4,2,49152]{2,1,0:T(2,128)(2,1)} %reshape.566), calls=%async_computation.3 | async-start | bytes 1572864 | tf_op jit(solution)/shard_map/all_to_all | solution.py:149
  200.0 14.3 %all-gather.1 = f32[8,2,804]{2,1,0:T(2,128)S(1)} all-gather(f32[1,2,804]{2,1,0:T(2,128)S(1)} %maximum_bitcast_fusion.1), channel_id=2, replica_groups=mesh['dp'=8,'ctx'=4] {'dp'}, dimensions={0}, use_global_device_ids=true | all-gather | bytes 57888 | tf_op jit(solution)/shard_map/all_gather | solution.py:117
  219.7 2.3 copy.272
  222.0 2.3 copy.274
  224.3 2.1 reshape.567
  226.4 1.5 copy.290
  228.8 1.5 copy.244
  230.2 2.3 squeeze.129
  232.6 2.1 convolution_convert_fusion.3
  234.7 2.7 convolution_convert_fusion
  237.4 1.8 convolution_convert_fusion.2
  240.8 1.4 broadcast.210
  242.2 13.7 %while.37 = (s32[]{:T(128)}, f32[12,128,64]{2,1,0:T(8,128)S(1)}, f32[2,12]{1,0:T(2,128)}, f32[2,12,128,64]{3,2,1,0:T(8,128)}, f32[2,12,128,64]{2,3,1,0:T(8,128)}...) while((s32[]{:T(128)}, f32[12,128,64]{2,1,0:T(8,128)S(1)}, ...), condition=%wide.region_8.9_spmd.clone, body=%wide.region_6.8_spmd.clone.sunk | while | flops 688132 | bytes 4327636 | solution.py:51
  243.1 1.3 dynamic_slice.149
  246.8 1.5 fusion.115
  249.9 1.3 dynamic_slice.149
  253.7 1.5 fusion.115
  255.9 3.8 %fusion.90 = f32[2,12,64,256]{3,2,1,0:T(8,128)S(1)} fusion(f32[2,12,128,64]{3,2,1,0:T(8,128)} %get-tuple-element.236, bf16[2,12,256,128]{3,2,1,0:T(8,128)(2,1)} %multiply_convert_fusion.2), kind=kOutput, calls=%fused_computation.192 | convolution fusion | flops 603979776 | bytes 3932160 | tf_op jit(solution)/shard_map/transpose(jvp(chsn,cshp->chnp))/dot_general | solution.py:42
  259.7 2.7 convolution_convert_fusion.1
  265.0 1.4 fusion.24
  266.5 5.7 %fusion.11 = (f32[2,12,256]{2,1,0:T(8,128)S(1)}, f32[2,12,256]{2,1,0:T(8,128)S(1)}, f32[2,256,256]{2,1,0:T(8,128)S(1)}) fusion(bf16[2,12,256,256]{3,2,1,0:T(8,128)(2,1)} %convolution_convert_fusion, f32[2,12,256]{2,1,0:T(8,128)S(1)} %copy-done.36, f32[2,256,256]{2,1,0:T(8,128)S(1)} %copy-done.25, pred[256,256]{1,0:T(8,128)(4,1)S(1)} %copy-done.38), kind=kLoop, calls=%fused_computation.26 | loop fusion | flops 18731008 | bytes 4333568 | tf_op jit(solution)/shard_map/transpose(jvp())/reduce_sum | solution.py:36
  272.4 3.8 %fusion.13 = (f32[2,256,128]{2,1,0:T(8,128)S(1)}, f32[2,12,256]{2,1,0:T(8,128)S(1)}, f32[2,12,256]{2,1,0:T(8,128)S(1)}, f32[2,256,128]{2,1,0:T(8,128)S(1)}) fusion(bf16[2,12,256,128]{3,2,1,0:T(8,128)(2,1)S(1)} %copy-done.22, f32[2,12,256]{2,1,0:T(8,128)S(1)} %copy-done.48, f32[2,256,128]{2,1,0:T(8,128)S(1)} %copy-done.30, f32[2,256,128]{2,1,0:T(8,128)S(1)} %copy-done.28, ...), kind=kLoop, calls=%fused_computation.32 | loop fusion | flops 7720960 | bytes 4292608 | tf_op jit(solution)/shard_map/transpose(jvp())/reduce_sum | solution.py:52
  276.8 5.0 %reduce-window.31 = f32[2,12,2,128]{3,1,2,0:T(8,128)S(1)} reduce-window(f32[2,12,2,128]{3,1,2,0:T(8,128)S(1)} %copy.261, f32[]{:T(128)} %constant.128.clone.1), window={size=1x1x1x128 pad=0_0x0_0x0_0x0_127}, to_apply=%region_15.16 | reduce-window | flops 780288 | bytes 49156 | tf_op jit(solution)/shard_map/reduce-window.2
  282.7 1.5 reduce.31
  285.0 4.2 %all-to-all-start.5 = ((bf16[4,2,768]{2,1,0:T(2,128)(2,1)}), bf16[4,2,768]{2,1,0:T(2,128)(2,1)S(1)}, u32[]{:S(2)}, u32[]{:S(2)}) async-start(bf16[4,2,768]{2,1,0:T(2,128)(2,1)} %reshape.570), calls=%async_computation.5 | async-start | bytes 24576 | tf_op jit(solution)/shard_map/all_to_all | solution.py:154
  292.6 1.6 copy.250
  294.2 5.5 %reduce.30 = bf16[512,768]{1,0:T(8,128)(2,1)S(1)} reduce(bf16[512,1,768]{2,1,0:T(2,128)(2,1)S(1)} %bitcast.221, bf16[]{:T(256)} %broadcast.249), dimensions={1}, to_apply=%bitcast.158.reduce_sub_computation | reduce | bytes 1572866
  301.0 2.2 reduce.32
  304.2 4.3 %all-to-all-start.6 = ((bf16[4,2,16384]{2,1,0:T(2,128)(2,1)}), bf16[4,2,16384]{2,1,0:T(2,128)(2,1)S(1)}, u32[]{:S(2)}, u32[]{:S(2)}) async-start(bf16[4,2,16384]{2,1,0:T(2,128)(2,1)} %reshape.572), calls=%async_computation.6 | async-start | bytes 524288 | tf_op jit(solution)/shard_map/all_to_all | solution.py:155
  308.6 40.7 %psum.7 = f32[3216]{0:T(1024)S(1)} all-reduce(f32[3216]{0:T(1024)S(1)} %pad_maximum_fusion), channel_id=1, replica_groups=mesh['dp'=8,'ctx'=4] {'dp','ctx'}, use_global_device_ids=true, to_apply=%region_27.28 | all-reduce | flops 3216 | bytes 25728 | tf_op jit(solution)/shard_map/psum | solution.py:167
  350.6 3.6 all-to-all-start.4
  358.9 5.6 %all-to-all-done.4 = bf16[4,2,49152]{2,1,0:T(2,128)(2,1)S(1)} async-done(((bf16[4,2,49152]{2,1,0:T(2,128)(2,1)}), bf16[4,2,49152]{2,1,0:T(2,128)(2,1)S(1)}, u32[]{:S(2)}, u32[]{:S(2)}) %all-to-all-start.4) | async-done | bytes 786464 | tf_op jit(solution)/shard_map/all_to_all | solution.py:153
  (316 shorter events, 59.9 us)
Async XLA Ops:
  3.3 49.1 %all-to-all-start.1 = ((bf16[4,2,768]{2,1,0:T(2,128)(2,1)}), bf16[4,2,768]{2,1,0:T(2,128)(2,1)S(1)}, u32[]{:S(2)}, u32[]{:S(2)}) async-start(bf16[4,2,768]{2,1,0:T(2,128)(2,1)} %reshape.560), calls=%async_computation.1 | async-start | bytes 24576 | tf_op jit(solution)/shard_map/all_to_all | solution.py:130
  9.3 23.2 %copy-start.73 = (f32[3,12]{1,0:T(4,128)}, f32[3,12]{1,0:T(4,128)S(1)}, u32[]{:S(2)}) copy-start(f32[3,12]{1,0:T(4,128)S(1)} %constant_dynamic-slice_fusion.4) | copy-start | bytes 436
  9.3 46.8 %copy-start.65 = (f32[12]{0:T(128)}, f32[12]{0:T(128)S(1)}, u32[]{:S(2)}) copy-start(f32[12]{0:T(128)S(1)} %get-tuple-element.511) | copy-start | bytes 148
  9.4 46.9 %copy-start.67 = (f32[12]{0:T(128)}, f32[12]{0:T(128)S(1)}, u32[]{:S(2)}) copy-start(f32[12]{0:T(128)S(1)} %get-tuple-element.512) | copy-start | bytes 148
  9.4 81.3 %copy-start.69 = (f32[12]{0:T(128)}, f32[12]{0:T(128)S(1)}, u32[]{:S(2)}) copy-start(f32[12]{0:T(128)S(1)} %get-tuple-element.510) | copy-start | bytes 148
  19.7 8.6 %copy-start.33 = (bf16[1,512,128]{2,1,0:T(8,128)(2,1)}, bf16[1,512,128]{2,1,0:T(8,128)(2,1)S(1)}, u32[]{:S(2)}) copy-start(bf16[1,512,128]{2,1,0:T(8,128)(2,1)S(1)} %all_gather.13) | copy-start | bytes 393220
  28.2 34.7 %copy-start.24 = (f32[2,256,256]{2,1,0:T(8,128)}, f32[2,256,256]{2,1,0:T(8,128)S(1)}, u32[]{:S(2)}) copy-start(f32[2,256,256]{2,1,0:T(8,128)S(1)} %fusion.87) | copy-start | bytes 1572868
  28.2 34.6 %copy-start.37 = (pred[256,256]{1,0:T(8,128)(4,1)}, pred[256,256]{1,0:T(8,128)(4,1)S(1)}, u32[]{:S(2)}) copy-start(pred[256,256]{1,0:T(8,128)(4,1)S(1)} %iota_compare_fusion) | copy-start | bytes 196612
  28.6 30.5 %copy-start.27 = (f32[2,256,128]{2,1,0:T(8,128)}, f32[2,256,128]{2,1,0:T(8,128)S(1)}, u32[]{:S(2)}) copy-start(f32[2,256,128]{2,1,0:T(8,128)S(1)} %convert_element_type.229) | copy-start | bytes 786436
  28.7 32.4 %copy-start.29 = (f32[2,256,128]{2,1,0:T(8,128)}, f32[2,256,128]{2,1,0:T(8,128)S(1)}, u32[]{:S(2)}) copy-start(f32[2,256,128]{2,1,0:T(8,128)S(1)} %convert_element_type.232) | copy-start | bytes 786436
  52.4 13.3 %all-to-all-start = ((bf16[4,2,49152]{2,1,0:T(2,128)(2,1)}), bf16[4,2,49152]{2,1,0:T(2,128)(2,1)S(1)}, u32[]{:S(2)}, u32[]{:S(2)}) async-start(bf16[4,2,49152]{2,1,0:T(2,128)(2,1)} %reshape.562), calls=%async_computation | async-start | bytes 1572864 | tf_op jit(solution)/shard_map/all_to_all | solution.py:129
  56.3 20.6 %copy-start.43 = (f32[2,256,12]{1,2,0:T(8,128)}, f32[2,256,12]{1,2,0:T(8,128)S(1)}, u32[]{:S(2)}) copy-start(f32[2,256,12]{1,2,0:T(8,128)S(1)} %get-tuple-element.503) | copy-start | bytes 73732
  58.9 4.0 %copy-start.41 = (f32[2,12,256]{2,0,1:T(2,128)}, f32[2,12,256]{2,0,1:T(2,128)S(1)}, u32[]{:S(2)}) copy-start(f32[2,12,256]{2,0,1:T(2,128)S(1)} %reduce_window_sum.56) | copy-start | bytes 73732
  59.1 3.7 %copy-start.45 = (f32[2,12,256]{2,1,0:T(8,128)}, f32[2,12,256]{2,1,0:T(8,128)S(1)}, u32[]{:S(2)}) copy-start(f32[2,12,256]{2,1,0:T(8,128)S(1)} %get-tuple-element.506) | copy-start | bytes 73732
  59.2 3.7 %copy-start.47 = (f32[2,12,256]{2,1,0:T(8,128)}, f32[2,12,256]{2,1,0:T(8,128)S(1)}, u32[]{:S(2)}) copy-start(f32[2,12,256]{2,1,0:T(8,128)S(1)} %get-tuple-element.507) | copy-start | bytes 73732
  59.2 3.7 %copy-start.35 = (f32[2,12,256]{2,1,0:T(8,128)}, f32[2,12,256]{2,1,0:T(8,128)S(1)}, u32[]{:S(2)}) copy-start(f32[2,12,256]{2,1,0:T(8,128)S(1)} %get-tuple-element.505) | copy-start | bytes 73732
  87.9 2.7 copy-start.56
  87.9 2.7 copy-start.5
  88.1 2.5 copy-start.19
  88.1 3.0 copy-start.2
  88.1 3.1 copy-start.8
  103.3 5.2 %copy-start.53 = (f32[3216]{0:T(1024)S(1)}, f32[3216]{0:T(1024)}, u32[]{:S(2)}) copy-start(f32[3216]{0:T(1024)} %param.23) | copy-start | bytes 38596
  103.3 5.3 %copy-start.58 = (s32[8]{0:T(128)S(1)}, s32[8]{0:T(128)}, u32[]{:S(2)}) copy-start(s32[8]{0:T(128)} %param.27) | copy-start | bytes 100
  104.3 21.0 %all-to-all-start.2 = ((bf16[4,2,49152]{2,1,0:T(2,128)(2,1)}), bf16[4,2,49152]{2,1,0:T(2,128)(2,1)}, u32[]{:S(2)}, u32[]{:S(2)}) async-start(bf16[4,2,49152]{2,1,0:T(2,128)(2,1)} %reshape.564), calls=%async_computation.2 | async-start | bytes 1572864 | tf_op jit(solution)/shard_map/all_to_all | solution.py:142
  119.3 3.8 %copy-start.77 = (s32[8]{0:T(128)S(1)}, s32[8]{0:T(128)}, u32[]{:S(2)}) copy-start(s32[8]{0:T(128)} %param.26) | copy-start | bytes 100
  172.4 27.6 %copy-start.63 = (f32[1,804]{1,0:T(1,128)S(1)}, f32[1,804]{1,0:T(1,128)}, u32[]{:S(2)}) copy-start(f32[1,804]{1,0:T(1,128)} %param.25) | copy-start | bytes 9652
  172.4 27.6 %copy-start.64 = (f32[1,804]{1,0:T(1,128)S(1)}, f32[1,804]{1,0:T(1,128)}, u32[]{:S(2)}) copy-start(f32[1,804]{1,0:T(1,128)} %param.24) | copy-start | bytes 9652
  173.4 50.9 %all-to-all-start.3 = ((bf16[4,2,49152]{2,1,0:T(2,128)(2,1)}), bf16[4,2,49152]{2,1,0:T(2,128)(2,1)S(1)}, u32[]{:S(2)}, u32[]{:S(2)}) async-start(bf16[4,2,49152]{2,1,0:T(2,128)(2,1)} %reshape.566), calls=%async_computation.3 | async-start | bytes 1572864 | tf_op jit(solution)/shard_map/all_to_all | solution.py:149
  232.5 4.9 %copy-start = (bf16[2,256,12,64]{1,0,3,2:T(2,128)(2,1)}, bf16[2,256,12,64]{1,0,3,2:T(2,128)(2,1)S(1)}, u32[]{:S(2)}) copy-start(bf16[2,256,12,64]{1,0,3,2:T(2,128)(2,1)S(1)} %squeeze.129) | copy-start | bytes 2359300
  232.6 2.1 copy-start.9
  234.7 2.8 copy-start.20
  242.2 3.3 copy-start.71
  249.0 3.4 copy-start.71
  255.9 3.8 %copy-start.10 = (bf16[2,256,12,64]{1,3,2,0:T(8,128)(2,1)S(1)}, bf16[2,256,12,64]{1,3,2,0:T(8,128)(2,1)}, u32[]{:S(2)}) copy-start(bf16[2,256,12,64]{1,3,2,0:T(8,128)(2,1)} %copy-done.7) | copy-start | bytes 2359300
  255.9 3.8 %copy-start.16 = (f32[2,12,128,64]{3,2,1,0:T(8,128)S(1)}, f32[2,12,128,64]{3,2,1,0:T(8,128)}, u32[]{:S(2)}) copy-start(f32[2,12,128,64]{3,2,1,0:T(8,128)} %get-tuple-element.236) | copy-start | bytes 2359300
  255.9 6.5 %copy-start.13 = (f32[1,128,3072]{1,0,2:T(1,128)S(1)}, f32[1,128,3072]{1,0,2:T(1,128)}, u32[]{:S(2)}) copy-start(f32[1,128,3072]{1,0,2:T(1,128)} %copy-done.12) | copy-start | bytes 4718596
  259.7 2.7 copy-start.18
  259.7 3.0 copy-start.3
  266.5 5.8 %copy-start.22 = (bf16[2,12,256,128]{3,2,1,0:T(8,128)(2,1)S(1)}, bf16[2,12,256,128]{3,2,1,0:T(8,128)(2,1)}, u32[]{:S(2)}) copy-start(bf16[2,12,256,128]{3,2,1,0:T(8,128)(2,1)} %convolution_convert_fusion.2) | copy-start | bytes 4718596
  266.5 5.8 %copy-start.23 = (bf16[2,12,256,128]{3,2,1,0:T(8,128)(2,1)S(1)}, bf16[2,12,256,128]{3,2,1,0:T(8,128)(2,1)}, u32[]{:S(2)}) copy-start(bf16[2,12,256,128]{3,2,1,0:T(8,128)(2,1)} %convolution_convert_fusion.1) | copy-start | bytes 4718596
  266.5 5.8 %copy-start.28 = (f32[2,256,128]{2,1,0:T(8,128)S(1)}, f32[2,256,128]{2,1,0:T(8,128)}, u32[]{:S(2)}) copy-start(f32[2,256,128]{2,1,0:T(8,128)} %copy-done.27) | copy-start | bytes 786436
  266.5 5.8 %copy-start.30 = (f32[2,256,128]{2,1,0:T(8,128)S(1)}, f32[2,256,128]{2,1,0:T(8,128)}, u32[]{:S(2)}) copy-start(f32[2,256,128]{2,1,0:T(8,128)} %copy-done.29) | copy-start | bytes 786436
  266.5 5.8 %copy-start.46 = (f32[2,12,256]{2,1,0:T(8,128)S(1)}, f32[2,12,256]{2,1,0:T(8,128)}, u32[]{:S(2)}) copy-start(f32[2,12,256]{2,1,0:T(8,128)} %copy-done.45) | copy-start | bytes 73732
  266.5 5.8 %copy-start.48 = (f32[2,12,256]{2,1,0:T(8,128)S(1)}, f32[2,12,256]{2,1,0:T(8,128)}, u32[]{:S(2)}) copy-start(f32[2,12,256]{2,1,0:T(8,128)} %copy-done.47) | copy-start | bytes 73732
  272.3 3.9 %copy-start.40 = (f32[2,12,2,128]{3,1,2,0:T(8,128)S(1)}, f32[2,12,2,128]{3,1,2,0:T(8,128)}, u32[]{:S(2)}) copy-start(f32[2,12,2,128]{3,1,2,0:T(8,128)} %copy-done.39) | copy-start | bytes 73732
  272.4 3.9 %copy-start.57 = (f32[2,12]{1,0:T(2,128)S(1)}, f32[2,12]{1,0:T(2,128)}, u32[]{:S(2)}) copy-start(f32[2,12]{1,0:T(2,128)} %copy-done.56) | copy-start | bytes 292
  272.4 3.9 %copy-start.60 = (f32[2,12,2]{1,2,0:T(2,128)S(1)}, f32[2,12,2]{1,2,0:T(2,128)}, u32[]{:S(2)}) copy-start(f32[2,12,2]{1,2,0:T(2,128)} %copy-done.59) | copy-start | bytes 580
  272.4 4.2 %copy-start.76 = (f32[2,12]{1,0:T(2,128)S(1)}, f32[2,12]{1,0:T(2,128)}, u32[]{:S(2)}) copy-start(f32[2,12]{1,0:T(2,128)} %get-tuple-element.237) | copy-start | bytes 292
  272.4 4.3 %copy-start.42 = (f32[2,12,256]{2,0,1:T(2,128)S(1)}, f32[2,12,256]{2,0,1:T(2,128)}, u32[]{:S(2)}) copy-start(f32[2,12,256]{2,0,1:T(2,128)} %copy-done.41) | copy-start | bytes 73732
  272.4 9.7 %copy-start.50 = (f32[2,256,12]{1,0,2:T(2,128)S(1)}, f32[2,256,12]{1,0,2:T(2,128)}, u32[]{:S(2)}) copy-start(f32[2,256,12]{1,0,2:T(2,128)} %copy-done.49) | copy-start | bytes 73732
  272.4 9.7 %copy-start.66 = (f32[12]{0:T(128)S(1)}, f32[12]{0:T(128)}, u32[]{:S(2)}) copy-start(f32[12]{0:T(128)} %copy-done.65) | copy-start | bytes 148
  272.4 9.7 %copy-start.68 = (f32[12]{0:T(128)S(1)}, f32[12]{0:T(128)}, u32[]{:S(2)}) copy-start(f32[12]{0:T(128)} %copy-done.67) | copy-start | bytes 148
  272.4 9.9 %copy-start.51 = (f32[1,4,128,12]{2,1,0,3:T(4,128)S(1)}, f32[1,4,128,12]{2,1,0,3:T(4,128)}, u32[]{:S(2)}) copy-start(f32[1,4,128,12]{2,1,0,3:T(4,128)} %copy.265) | copy-start | bytes 73732
  276.2 13.0 %copy-start.34 = (bf16[1,512,128]{2,1,0:T(8,128)(2,1)S(1)}, bf16[1,512,128]{2,1,0:T(8,128)(2,1)}, u32[]{:S(2)}) copy-start(bf16[1,512,128]{2,1,0:T(8,128)(2,1)} %copy-done.33) | copy-start | bytes 393220
  276.2 13.4 %copy-start.32 = (bf16[1,512,128]{2,1,0:T(8,128)(2,1)S(1)}, bf16[1,512,128]{2,1,0:T(8,128)(2,1)}, u32[]{:S(2)}) copy-start(bf16[1,512,128]{2,1,0:T(8,128)(2,1)} %copy-done.31) | copy-start | bytes 393220
  282.7 8.5 %copy-start.26 = (bf16[2,256,12,64]{1,3,2,0:T(8,128)(2,1)S(1)}, bf16[2,256,12,64]{1,3,2,0:T(8,128)(2,1)}, u32[]{:S(2)}) copy-start(bf16[2,256,12,64]{1,3,2,0:T(8,128)(2,1)} %get-tuple-element.492) | copy-start | bytes 2359300
  285.0 19.2 %all-to-all-start.5 = ((bf16[4,2,768]{2,1,0:T(2,128)(2,1)}), bf16[4,2,768]{2,1,0:T(2,128)(2,1)S(1)}, u32[]{:S(2)}, u32[]{:S(2)}) async-start(bf16[4,2,768]{2,1,0:T(2,128)(2,1)} %reshape.570), calls=%async_computation.5 | async-start | bytes 24576 | tf_op jit(solution)/shard_map/all_to_all | solution.py:154
  300.6 7.9 %copy-start.55 = (f32[3072]{0:T(1024)S(1)}, f32[3072]{0:T(1024)}, u32[]{:S(2)}) copy-start(f32[3072]{0:T(1024)} %get-tuple-element.436) | copy-start | bytes 36868
  301.0 53.2 %copy-start.61 = (f32[804]{0:T(1024)S(1)}, f32[804]{0:T(1024)}, u32[]{:S(2)}) copy-start(f32[804]{0:T(1024)} %get-tuple-element.532) | copy-start | bytes 9652
  301.0 53.2 %copy-start.62 = (f32[804]{0:T(1024)S(1)}, f32[804]{0:T(1024)}, u32[]{:S(2)}) copy-start(f32[804]{0:T(1024)} %get-tuple-element.533) | copy-start | bytes 9652
  303.3 52.8 %copy-start.52 = (f32[3216]{0:T(1024)S(1)}, f32[3216]{0:T(1024)}, u32[]{:S(2)}) copy-start(f32[3216]{0:T(1024)} %get-tuple-element.445) | copy-start | bytes 38596
  303.3 52.8 %copy-start.54 = (f32[3216]{0:T(1024)S(1)}, f32[3216]{0:T(1024)}, u32[]{:S(2)}) copy-start(f32[3216]{0:T(1024)} %param.23) | copy-start | bytes 38596
  304.2 46.4 %all-to-all-start.6 = ((bf16[4,2,16384]{2,1,0:T(2,128)(2,1)}), bf16[4,2,16384]{2,1,0:T(2,128)(2,1)S(1)}, u32[]{:S(2)}, u32[]{:S(2)}) async-start(bf16[4,2,16384]{2,1,0:T(2,128)(2,1)} %reshape.572), calls=%async_computation.6 | async-start | bytes 524288 | tf_op jit(solution)/shard_map/all_to_all | solution.py:155
  350.6 13.8 %all-to-all-start.4 = ((bf16[4,2,49152]{2,1,0:T(2,128)(2,1)}), bf16[4,2,49152]{2,1,0:T(2,128)(2,1)S(1)}, u32[]{:S(2)}, u32[]{:S(2)}) async-start(bf16[4,2,49152]{2,1,0:T(2,128)(2,1)} %reshape.568), calls=%async_computation.4 | async-start | bytes 1572864 | tf_op jit(solution)/shard_map/all_to_all | solution.py:153
  (26 other events, 33.6 us)
where the time goes:
time: 374 us; the launch traced here: 367 us
  other arithmetic  105 us (28%)
  local copies, waits for them, and re-layouts  99.3 us (27%)
  blocking collectives  72.3 us (19%)
  between operations  34.9 us (9%)
  starting transfers between devices  29.3 us (8%)
  matrix products  20.4 us (5%)
  waiting for transfers between devices  5.57 us (1%)
    unnamed x10, other arithmetic  52.7 us
    psum x1, blocking collectives, on_device(): gradient = lax.psum(grad_part, ('dp', 'ctx'))  40.7 us
    unnamed x171, local copies, waits for them, and re-layouts  40.3 us
    all_gather x1, blocking collectives, on_device(): lax.all_gather(jnp.stack([adam_mean[0], adam_square[0]]), 'dp', axis=0)  14.3 us
    convert_element_type x1, local copies, waits for them, and re-layouts, norm_backward(): d_y = (d_gated * (gate_f * sigma)).astype(jnp.bfloat16)  13 us
    all_gather x1, blocking collectives, on_device(): lax.all_gather(b_input, 'ctx', axis=1, tiled=True)  9.13 us
    dot_general x3, matrix products, ssd_group(): jnp.einsum('chsn,cshp->chnp', b_decayed, scaled, precision=highest)  8.29 us
    all_gather x1, blocking collectives, on_device(): lax.all_gather(c_input, 'ctx', axis=1, tiled=True)  8.23 us
  transfers between devices with their start and end apart: 7, of which 1 were waited for; matrix products, arithmetic and copies ran while one was open for 19% of the time, Pallas kernels for 0%

commit v1 on v0

--- a/solution.py
+++ b/solution.py
@@ -164,7 +164,7 @@
         jnp.zeros((3, heads_all), jnp.float32), head_grads, (0, first)
     )
     grad_part = jnp.concatenate([full_heads.reshape(-1), d_gain])
-    gradient = lax.psum(grad_part, ("dp", "ctx"))
+    gradient = jnp.sum(lax.all_gather(grad_part, ("dp", "ctx")), axis=0)
     grad_norm = jnp.sqrt(jnp.sum(gradient * gradient))
     shrink = jnp.minimum(1.0, clip_norm / (grad_norm + 1e-06))
     owners = lax.axis_size("dp")

time: 374 us -> 475 us (1.27)
  waiting for transfers between devices: 5.57 us -> 128 us
  blocking collectives: 72.3 us -> 31.6 us
  between operations: 34.9 us -> 48.2 us
  local copies, waits for them, and re-layouts: 99.3 us -> 105 us
    unnamed x0 -> x2, waiting for transfers between devices: none -> 125 us
    psum x1 -> x0, blocking collectives: 40.7 us -> none  [on_device(): gradient = lax.psum(grad_part, ('dp', 'ctx'))]
    all_to_all x1, waiting for transfers between devices: 5.56 us -> 0.01 us  [on_device(): lax.all_to_all(d_x[None], 'ctx', split_axis=1, concat_axis=2, tiled=True)]
    unnamed x171 -> x176, local copies, waits for them, and re-layouts: 40.3 us -> 43.2 us
    unnamed x10 -> x11, other arithmetic: 52.7 us -> 52.9 us
  transfers between devices with their start and end apart: 7 -> 8, of which waited for: 1 -> 2; matrix products, arithmetic and copies ran while one was open for 19% -> 16% of each run, Pallas kernels for 0% -> 0%
where the time goes in v1:
time: 475 us; the launch traced here: 467 us
  waiting for transfers between devices  128 us (27%)
  local copies, waits for them, and re-layouts  105 us (22%)
  other arithmetic  104 us (22%)
  between operations  48.2 us (10%)
  blocking collectives  31.6 us (7%)
  starting transfers between devices  30.1 us (6%)
  matrix products  20.3 us (4%)
    unnamed x2, waiting for transfers between devices  125 us
    unnamed x11, other arithmetic  52.9 us
    unnamed x176, local copies, waits for them, and re-layouts  43.2 us
    all_gather x1, blocking collectives, on_device(): lax.all_gather(jnp.stack([adam_mean[0], adam_square[0]]), 'dp', axis=0)  14.3 us
    convert_element_type x1, local copies, waits for them, and re-layouts, norm_backward(): d_y = (d_gated * (gate_f * sigma)).astype(jnp.bfloat16)  13 us
  transfers between devices with their start and end apart: 8, of which 2 were waited for; matrix products, arithmetic and copies ran while one was open for 16% of the time, Pallas kernels for 0%

profile of v1, /device:TPU:0, one launch (start us, length us, event | category | flops | bytes accessed | tf_op | source)
XLA Modules:
  0.0 467.4 jit_solution(18158994507360204475)
XLA Ops:
  9.8 5.2 %all-to-all-start.1 = ((bf16[4,2,768]{2,1,0:T(2,128)(2,1)}), bf16[4,2,768]{2,1,0:T(2,128)(2,1)S(1)}, u32[]{:S(2)}, u32[]{:S(2)}) async-start(bf16[4,2,768]{2,1,0:T(2,128)(2,1)} %reshape.563), calls=%async_computation.1 | async-start | bytes 24576 | tf_op jit(solution)/shard_map/all_to_all | solution.py:130
  17.1 9.1 %all_gather.19 = bf16[1,512,128]{2,1,0:T(8,128)(2,1)S(1)} all-gather(bf16[1,128,128]{2,1,0:T(8,128)(2,1)} %param.19), channel_id=1, replica_groups=mesh['dp'=8,'ctx'=4] {'ctx'}, dimensions={1}, use_global_device_ids=true | all-gather | bytes 163840 | tf_op jit(solution)/shard_map/all_gather | solution.py:110
  26.2 8.2 %all_gather.18 = bf16[1,512,128]{2,1,0:T(8,128)(2,1)S(1)} all-gather(bf16[1,128,128]{2,1,0:T(8,128)(2,1)} %param.20), channel_id=1, replica_groups=mesh['dp'=8,'ctx'=4] {'ctx'}, dimensions={1}, use_global_device_ids=true | all-gather | bytes 163840 | tf_op jit(solution)/shard_map/all_gather | solution.py:111
  35.2 3.8 copy.220
  39.0 17.9 %reduce.27 = bf16[3072,128]{1,0:T(8,128)(2,1)} reduce(bf16[3072,1,128]{2,1,0:T(2,128)(2,1)S(1)} %bitcast.223, bf16[]{:T(256)} %broadcast.250), dimensions={1}, to_apply=%bitcast.152.reduce_sub_computation | reduce | bytes 1572866
  56.9 2.0 reshape.565
  58.9 4.4 all-to-all-start
  66.3 1.8 multiply_convert_fusion.2
  68.2 1.8 multiply_convert_fusion.1
  70.1 2.8 multiply_convert_fusion
  72.9 2.4 reshape.566
  75.3 1.7 bitcast_convert_fusion
  78.2 2.2 copy.221
  80.4 2.6 reshape.535
  85.0 1.8 fusion.88
  87.0 6.9 %while.36 = (s32[]{:T(128)}, f32[12,128,64]{2,1,0:T(8,128)S(1)}, f32[2,12,128,64]{3,2,1,0:T(8,128)S(1)}, f32[2,12]{1,0:T(2,128)S(1)}, f32[2,12,1,1]{1,3,2,0:T(1,...) while((s32[]{:T(128)}, f32[12,128,64]{2,1,0:T(8,128)S(1)}, ...), condition=%wide.region_3.4_spmd.clone, body=%wide.region_2.3_spmd.clone.sunk | while | flops 589827 | bytes 5899176 | solution.py:51
  94.1 2.5 fusion.89
  99.1 1.4 convert_element_type.235
  100.5 3.9 copy.238
  104.4 6.3 %reduce.28 = bf16[512,768]{1,0:T(8,128)(2,1)} reduce(bf16[512,1,768]{2,1,0:T(2,128)(2,1)S(1)} %bitcast.217, bf16[]{:T(256)} %broadcast.250), dimensions={1}, to_apply=%bitcast.154.reduce_sub_computation | reduce | bytes 1572866
  110.8 2.0 reshape.567
  112.8 4.5 all-to-all-start.2
  128.0 1.5 copy.241
  129.6 2.3 copy.242
  132.7 1.3 fusion.79
  134.0 3.7 reshape.568
  137.8 1.5 copy.239
  139.3 1.3 convert_bitcast_fusion
  140.6 3.0 copy.240
  143.6 2.0 multiply_reduce_fusion.1
  145.7 1.5 fusion.21
  147.2 2.5 fusion.30
  149.7 13.0 %copy.372 = bf16[1,128,3072]{1,0,2:T(2,128)(2,1)} copy(bf16[1,128,3072]{1,2,0:T(8,128)(2,1)S(1)} %get-tuple-element.489) | data formatting | bytes 1572864 | tf_op jit(solution)/shard_map/convert_element_type | solution.py:76
  162.7 18.5 %reduce.29 = bf16[3072,128]{1,0:T(8,128)(2,1)S(1)} reduce(bf16[3072,1,128]{2,1,0:T(2,128)(2,1)} %bitcast.219, bf16[]{:T(256)} %broadcast.250), dimensions={1}, to_apply=%bitcast.190.reduce_sub_computation | reduce | bytes 1572866
  182.2 4.2 all-to-all-start.3
  208.8 14.3 %all-gather.2 = f32[8,2,804]{2,1,0:T(2,128)S(1)} all-gather(f32[1,2,804]{2,1,0:T(2,128)S(1)} %maximum_bitcast_fusion.1), channel_id=2, replica_groups=mesh['dp'=8,'ctx'=4] {'dp'}, dimensions={0}, use_global_device_ids=true | all-gather | bytes 57888 | tf_op jit(solution)/shard_map/all_gather | solution.py:117
  228.5 2.3 copy.272
  230.8 2.3 copy.274
  233.1 2.1 reshape.570
  235.1 1.5 copy.290
  237.5 1.5 copy.244
  239.0 2.3 squeeze.129
  241.3 2.1 convolution_convert_fusion.3
  243.5 2.7 convolution_convert_fusion
  246.2 1.8 convolution_convert_fusion.2
  249.5 1.4 broadcast.210
  250.9 13.6 %while.37 = (s32[]{:T(128)}, f32[12,128,64]{2,1,0:T(8,128)S(1)}, f32[2,12]{1,0:T(2,128)}, f32[2,12,128,64]{3,2,1,0:T(8,128)}, f32[2,12,128,64]{2,3,1,0:T(8,128)}...) while((s32[]{:T(128)}, f32[12,128,64]{2,1,0:T(8,128)S(1)}, ...), condition=%wide.region_8.9_spmd.clone, body=%wide.region_6.8_spmd.clone.sunk | while | flops 688132 | bytes 4327636 | solution.py:51
  255.5 1.5 fusion.115
  262.4 1.5 fusion.115
  264.6 3.8 fusion.90
  268.4 2.7 convolution_convert_fusion.1
  273.7 1.4 fusion.24
  275.9 5.9 %fusion.11 = (f32[2,12,256]{2,1,0:T(8,128)S(1)}, f32[2,12,256]{2,1,0:T(8,128)S(1)}, f32[2,256,256]{2,1,0:T(8,128)}) fusion(bf16[2,12,256,256]{3,2,1,0:T(8,128)(2,1)S(1)} %copy-done.17, f32[2,12,256]{2,1,0:T(8,128)S(1)} %copy-done.38, f32[2,256,256]{2,1,0:T(8,128)} %copy-done.26, pred[256,256]{1,0:T(8,128)(4,1)S(1)} %copy-done.40), kind=kLoop, calls=%fused_computation.26 | loop fusion | flops 18731008 | bytes 4333568 | tf_op jit(solution)/shard_map/transpose(jvp())/reduce_sum | solution.py:36
  281.9 3.8 fusion.13
  286.3 5.0 %reduce-window.31 = f32[2,12,2,128]{3,1,2,0:T(8,128)S(1)} reduce-window(f32[2,12,2,128]{3,1,2,0:T(8,128)S(1)} %copy.261, f32[]{:T(128)} %constant.128.clone.1), window={size=1x1x1x128 pad=0_0x0_0x0_0x0_127}, to_apply=%region_15.16 | reduce-window | flops 780288 | bytes 49156 | tf_op jit(solution)/shard_map/reduce-window.2
  292.2 1.5 reduce.31
  294.6 4.2 all-to-all-start.5
  301.9 1.6 copy.250
  303.5 5.5 %reduce.30 = bf16[512,768]{1,0:T(8,128)(2,1)S(1)} reduce(bf16[512,1,768]{2,1,0:T(2,128)(2,1)S(1)} %bitcast.221, bf16[]{:T(256)} %broadcast.250), dimensions={1}, to_apply=%bitcast.158.reduce_sub_computation | reduce | bytes 1572866
  310.4 2.2 reduce.32
  313.6 4.2 all-to-all-start.6
  320.2 2.9 all-to-all-done.6
  323.1 3.5 all-to-all-start.4
  327.7 125.0 %all-reduce.6.cloned.1.call-done = f32[102912]{0:T(1024)} async-done(((f32[102912]{0:T(1024)}), f32[102912]{0:T(1024)}) %all-reduce.6.cloned.1.call-update) | async-done | bytes 411664
  (325 shorter events, 63.9 us)
Async XLA Ops:
  9.8 49.0 %all-to-all-start.1 = ((bf16[4,2,768]{2,1,0:T(2,128)(2,1)}), bf16[4,2,768]{2,1,0:T(2,128)(2,1)S(1)}, u32[]{:S(2)}, u32[]{:S(2)}) async-start(bf16[4,2,768]{2,1,0:T(2,128)(2,1)} %reshape.563), calls=%async_computation.1 | async-start | bytes 24576 | tf_op jit(solution)/shard_map/all_to_all | solution.py:130
  15.9 23.1 %copy-start.75 = (f32[3,12]{1,0:T(4,128)}, f32[3,12]{1,0:T(4,128)S(1)}, u32[]{:S(2)}) copy-start(f32[3,12]{1,0:T(4,128)S(1)} %constant_dynamic-slice_fusion.4) | copy-start | bytes 436
  15.9 47.5 %copy-start.67 = (f32[12]{0:T(128)}, f32[12]{0:T(128)S(1)}, u32[]{:S(2)}) copy-start(f32[12]{0:T(128)S(1)} %get-tuple-element.511) | copy-start | bytes 148
  15.9 47.5 %copy-start.69 = (f32[12]{0:T(128)}, f32[12]{0:T(128)S(1)}, u32[]{:S(2)}) copy-start(f32[12]{0:T(128)S(1)} %get-tuple-element.512) | copy-start | bytes 148
  15.9 80.7 %copy-start.71 = (f32[12]{0:T(128)}, f32[12]{0:T(128)S(1)}, u32[]{:S(2)}) copy-start(f32[12]{0:T(128)S(1)} %get-tuple-element.510) | copy-start | bytes 148
  26.2 8.6 %copy-start.34 = (bf16[1,512,128]{2,1,0:T(8,128)(2,1)}, bf16[1,512,128]{2,1,0:T(8,128)(2,1)S(1)}, u32[]{:S(2)}) copy-start(bf16[1,512,128]{2,1,0:T(8,128)(2,1)S(1)} %all_gather.19) | copy-start | bytes 393220
  34.7 35.3 %copy-start.26 = (f32[2,256,256]{2,1,0:T(8,128)}, f32[2,256,256]{2,1,0:T(8,128)S(1)}, u32[]{:S(2)}) copy-start(f32[2,256,256]{2,1,0:T(8,128)S(1)} %fusion.87) | copy-start | bytes 1572868
  34.7 35.3 %copy-start.39 = (pred[256,256]{1,0:T(8,128)(4,1)}, pred[256,256]{1,0:T(8,128)(4,1)S(1)}, u32[]{:S(2)}) copy-start(pred[256,256]{1,0:T(8,128)(4,1)S(1)} %iota_compare_fusion) | copy-start | bytes 196612
  35.1 31.2 %copy-start.28 = (f32[2,256,128]{2,1,0:T(8,128)}, f32[2,256,128]{2,1,0:T(8,128)S(1)}, u32[]{:S(2)}) copy-start(f32[2,256,128]{2,1,0:T(8,128)S(1)} %convert_element_type.229) | copy-start | bytes 786436
  35.2 33.0 %copy-start.30 = (f32[2,256,128]{2,1,0:T(8,128)}, f32[2,256,128]{2,1,0:T(8,128)S(1)}, u32[]{:S(2)}) copy-start(f32[2,256,128]{2,1,0:T(8,128)S(1)} %convert_element_type.232) | copy-start | bytes 786436
  58.9 14.0 %all-to-all-start = ((bf16[4,2,49152]{2,1,0:T(2,128)(2,1)}), bf16[4,2,49152]{2,1,0:T(2,128)(2,1)}, u32[]{:S(2)}, u32[]{:S(2)}) async-start(bf16[4,2,49152]{2,1,0:T(2,128)(2,1)} %reshape.565), calls=%async_computation | async-start | bytes 1572864 | tf_op jit(solution)/shard_map/all_to_all | solution.py:129
  63.5 19.5 %copy-start.45 = (f32[2,256,12]{1,2,0:T(8,128)}, f32[2,256,12]{1,2,0:T(8,128)S(1)}, u32[]{:S(2)}) copy-start(f32[2,256,12]{1,2,0:T(8,128)S(1)} %get-tuple-element.503) | copy-start | bytes 73732
  65.1 4.9 %copy-start.41 = (f32[2,12,2,128]{3,1,2,0:T(8,128)}, f32[2,12,2,128]{3,1,2,0:T(8,128)S(1)}, u32[]{:S(2)}) copy-start(f32[2,12,2,128]{3,1,2,0:T(8,128)S(1)} %reduce-window.24) | copy-start | bytes 73732
  66.0 4.0 copy-start.43
  66.3 3.7 copy-start.47
  66.3 3.7 copy-start.49
  66.3 3.7 copy-start.37
  93.9 2.7 copy-start.5
  94.1 3.0 copy-start.2
  94.1 3.1 copy-start.8
  110.8 6.5 %copy-start.55 = (f32[3216]{0:T(1024)S(1)}, f32[3216]{0:T(1024)}, u32[]{:S(2)}) copy-start(f32[3216]{0:T(1024)} %param.23) | copy-start | bytes 38596
  110.8 6.6 %copy-start.60 = (s32[8]{0:T(128)S(1)}, s32[8]{0:T(128)}, u32[]{:S(2)}) copy-start(s32[8]{0:T(128)} %param.27) | copy-start | bytes 100
  112.8 21.3 %all-to-all-start.2 = ((bf16[4,2,49152]{2,1,0:T(2,128)(2,1)}), bf16[4,2,49152]{2,1,0:T(2,128)(2,1)}, u32[]{:S(2)}, u32[]{:S(2)}) async-start(bf16[4,2,49152]{2,1,0:T(2,128)(2,1)} %reshape.567), calls=%async_computation.2 | async-start | bytes 1572864 | tf_op jit(solution)/shard_map/all_to_all | solution.py:142
  128.0 3.8 copy-start.79
  181.1 27.6 %copy-start.65 = (f32[1,804]{1,0:T(1,128)S(1)}, f32[1,804]{1,0:T(1,128)}, u32[]{:S(2)}) copy-start(f32[1,804]{1,0:T(1,128)} %param.25) | copy-start | bytes 9652
  181.1 27.6 %copy-start.66 = (f32[1,804]{1,0:T(1,128)S(1)}, f32[1,804]{1,0:T(1,128)}, u32[]{:S(2)}) copy-start(f32[1,804]{1,0:T(1,128)} %param.24) | copy-start | bytes 9652
  182.2 50.9 %all-to-all-start.3 = ((bf16[4,2,49152]{2,1,0:T(2,128)(2,1)}), bf16[4,2,49152]{2,1,0:T(2,128)(2,1)S(1)}, u32[]{:S(2)}, u32[]{:S(2)}) async-start(bf16[4,2,49152]{2,1,0:T(2,128)(2,1)} %reshape.569), calls=%async_computation.3 | async-start | bytes 1572864 | tf_op jit(solution)/shard_map/all_to_all | solution.py:149
  241.3 4.9 %copy-start = (bf16[2,256,12,64]{1,0,3,2:T(2,128)(2,1)}, bf16[2,256,12,64]{1,0,3,2:T(2,128)(2,1)S(1)}, u32[]{:S(2)}) copy-start(bf16[2,256,12,64]{1,0,3,2:T(2,128)(2,1)S(1)} %squeeze.129) | copy-start | bytes 2359300
  243.5 2.8 copy-start.21
  250.9 3.3 copy-start.73
  257.7 3.4 copy-start.73
  264.6 3.8 copy-start.10
  264.6 3.8 copy-start.16
  264.6 6.5 %copy-start.13 = (f32[1,128,3072]{1,0,2:T(1,128)S(1)}, f32[1,128,3072]{1,0,2:T(1,128)}, u32[]{:S(2)}) copy-start(f32[1,128,3072]{1,0,2:T(1,128)} %copy-done.12) | copy-start | bytes 4718596
  268.4 2.7 copy-start.19
  268.4 2.9 copy-start.3
  275.8 6.0 %copy-start.23 = (bf16[2,12,256,128]{3,2,1,0:T(8,128)(2,1)S(1)}, bf16[2,12,256,128]{3,2,1,0:T(8,128)(2,1)}, u32[]{:S(2)}) copy-start(bf16[2,12,256,128]{3,2,1,0:T(8,128)(2,1)} %convolution_convert_fusion.2) | copy-start | bytes 4718596
  275.8 6.0 %copy-start.24 = (bf16[2,12,256,128]{3,2,1,0:T(8,128)(2,1)S(1)}, bf16[2,12,256,128]{3,2,1,0:T(8,128)(2,1)}, u32[]{:S(2)}) copy-start(bf16[2,12,256,128]{3,2,1,0:T(8,128)(2,1)} %convolution_convert_fusion.1) | copy-start | bytes 4718596
  275.8 6.0 %copy-start.29 = (f32[2,256,128]{2,1,0:T(8,128)S(1)}, f32[2,256,128]{2,1,0:T(8,128)}, u32[]{:S(2)}) copy-start(f32[2,256,128]{2,1,0:T(8,128)} %copy-done.28) | copy-start | bytes 786436
  275.8 6.0 %copy-start.31 = (f32[2,256,128]{2,1,0:T(8,128)S(1)}, f32[2,256,128]{2,1,0:T(8,128)}, u32[]{:S(2)}) copy-start(f32[2,256,128]{2,1,0:T(8,128)} %copy-done.30) | copy-start | bytes 786436
  275.9 6.0 %copy-start.48 = (f32[2,12,256]{2,1,0:T(8,128)S(1)}, f32[2,12,256]{2,1,0:T(8,128)}, u32[]{:S(2)}) copy-start(f32[2,12,256]{2,1,0:T(8,128)} %copy-done.47) | copy-start | bytes 73732
  275.9 6.0 %copy-start.50 = (f32[2,12,256]{2,1,0:T(8,128)S(1)}, f32[2,12,256]{2,1,0:T(8,128)}, u32[]{:S(2)}) copy-start(f32[2,12,256]{2,1,0:T(8,128)} %copy-done.49) | copy-start | bytes 73732
  281.9 3.9 copy-start.42
  281.9 3.9 copy-start.59
  281.9 3.9 copy-start.62
  281.9 4.2 copy-start.78
  281.9 4.3 copy-start.44
  281.9 9.7 %copy-start.52 = (f32[2,256,12]{1,0,2:T(2,128)S(1)}, f32[2,256,12]{1,0,2:T(2,128)}, u32[]{:S(2)}) copy-start(f32[2,256,12]{1,0,2:T(2,128)} %copy-done.51) | copy-start | bytes 73732
  281.9 9.7 %copy-start.68 = (f32[12]{0:T(128)S(1)}, f32[12]{0:T(128)}, u32[]{:S(2)}) copy-start(f32[12]{0:T(128)} %copy-done.67) | copy-start | bytes 148
  281.9 9.7 %copy-start.70 = (f32[12]{0:T(128)S(1)}, f32[12]{0:T(128)}, u32[]{:S(2)}) copy-start(f32[12]{0:T(128)} %copy-done.69) | copy-start | bytes 148
  281.9 10.0 %copy-start.53 = (f32[1,4,128,12]{2,1,0,3:T(4,128)S(1)}, f32[1,4,128,12]{2,1,0,3:T(4,128)}, u32[]{:S(2)}) copy-start(f32[1,4,128,12]{2,1,0,3:T(4,128)} %copy.265) | copy-start | bytes 73732
  285.7 13.1 %copy-start.25 = (f32[2,256,256]{2,1,0:T(8,128)S(1)}, f32[2,256,256]{2,1,0:T(8,128)}, u32[]{:S(2)}) copy-start(f32[2,256,256]{2,1,0:T(8,128)} %get-tuple-element.435) | copy-start | bytes 1572868
  285.7 13.0 %copy-start.35 = (bf16[1,512,128]{2,1,0:T(8,128)(2,1)S(1)}, bf16[1,512,128]{2,1,0:T(8,128)(2,1)}, u32[]{:S(2)}) copy-start(bf16[1,512,128]{2,1,0:T(8,128)(2,1)} %copy-done.34) | copy-start | bytes 393220
  285.7 13.4 %copy-start.33 = (bf16[1,512,128]{2,1,0:T(8,128)(2,1)S(1)}, bf16[1,512,128]{2,1,0:T(8,128)(2,1)}, u32[]{:S(2)}) copy-start(bf16[1,512,128]{2,1,0:T(8,128)(2,1)} %copy-done.32) | copy-start | bytes 393220
  292.2 8.4 %copy-start.27 = (bf16[2,256,12,64]{1,3,2,0:T(8,128)(2,1)S(1)}, bf16[2,256,12,64]{1,3,2,0:T(8,128)(2,1)}, u32[]{:S(2)}) copy-start(bf16[2,256,12,64]{1,3,2,0:T(8,128)(2,1)} %get-tuple-element.492) | copy-start | bytes 2359300
  294.6 19.0 %all-to-all-start.5 = ((bf16[4,2,768]{2,1,0:T(2,128)(2,1)}), bf16[4,2,768]{2,1,0:T(2,128)(2,1)S(1)}, u32[]{:S(2)}, u32[]{:S(2)}) async-start(bf16[4,2,768]{2,1,0:T(2,128)(2,1)} %reshape.573), calls=%async_computation.5 | async-start | bytes 24576 | tf_op jit(solution)/shard_map/all_to_all | solution.py:154
  310.0 8.1 %copy-start.57 = (f32[3072]{0:T(1024)S(1)}, f32[3072]{0:T(1024)}, u32[]{:S(2)}) copy-start(f32[3072]{0:T(1024)} %get-tuple-element.436) | copy-start | bytes 36868
  313.6 9.6 %all-to-all-start.6 = ((bf16[4,2,16384]{2,1,0:T(2,128)(2,1)}), bf16[4,2,16384]{2,1,0:T(2,128)(2,1)S(1)}, u32[]{:S(2)}, u32[]{:S(2)}) async-start(bf16[4,2,16384]{2,1,0:T(2,128)(2,1)} %reshape.575), calls=%async_computation.6 | async-start | bytes 524288 | tf_op jit(solution)/shard_map/all_to_all | solution.py:155
  317.8 134.9 %all-reduce.6.cloned.1.call-start = ((), (), s32[]{:S(2)}) async-start(), calls=%async_computation.7 | async-start | bytes 827392
  323.1 134.7 %all-to-all-start.4 = ((bf16[4,2,49152]{2,1,0:T(2,128)(2,1)}), bf16[4,2,49152]{2,1,0:T(2,128)(2,1)S(1)}, u32[]{:S(2)}, u32[]{:S(2)}) async-start(bf16[4,2,49152]{2,1,0:T(2,128)(2,1)} %reshape.571), calls=%async_computation.4 | async-start | bytes 1572864 | tf_op jit(solution)/shard_map/all_to_all | solution.py:153
  326.6 128.7 %copy-start.63 = (f32[804]{0:T(1024)S(1)}, f32[804]{0:T(1024)}, u32[]{:S(2)}) copy-start(f32[804]{0:T(1024)} %get-tuple-element.532) | copy-start | bytes 9652
  326.6 128.7 %copy-start.64 = (f32[804]{0:T(1024)S(1)}, f32[804]{0:T(1024)}, u32[]{:S(2)}) copy-start(f32[804]{0:T(1024)} %get-tuple-element.533) | copy-start | bytes 9652
  326.7 130.6 %copy-start.54 = (f32[3216]{0:T(1024)S(1)}, f32[3216]{0:T(1024)}, u32[]{:S(2)}) copy-start(f32[3216]{0:T(1024)} %get-tuple-element.445) | copy-start | bytes 38596
  326.7 130.6 %copy-start.56 = (f32[3216]{0:T(1024)S(1)}, f32[3216]{0:T(1024)}, u32[]{:S(2)}) copy-start(f32[3216]{0:T(1024)} %param.23) | copy-start | bytes 38596
  (29 other events, 42.6 us)
Sparse Core Ops, SparseCore 0:
  323.9 128.7 all-reduce.5
